TPU v7x, 256 devices: a whole 4x4x8 slice. The times are simulated.
256 devices in a mesh: row: 16 (over z_hi, y, core), col: 4 (over z_lo), pblk: 4 (over x).
Axes of the slice: x: 4, y: 4, z: 8 (z_hi: 2, z_lo: 4; z = z_hi * 4 + z_lo), core: 2. Of those that a mesh axis runs over, the one named last changes fastest.
Arguments:
- left_feat: int32 [2048, 256], P(('row', 'col', 'pblk')), may hold values from 0 to 255
- right_feat: int32 [4, 4, 64, 256], P('col', 'pblk', 'row'), may hold values from 0 to 255
- embed: bfloat16 [1024, 256], replicated, may hold values from -12 to 12
- conv_w: bfloat16 [8, 768, 256], replicated, may hold values from -0.01953125 to 0.01953125
- head: float32 [256], replicated, may hold values from -0.078125 to 0.078125
- assign: int32 [8], replicated, may hold values from 0 to 3, as said below
- proj_delta: bfloat16 [4, 256, 128], replicated, may hold values from -0.375 to 0.375
- proj_input: bfloat16 [4, 768, 128], replicated, may hold values from -0.21875 to 0.21875
Outputs:
- kernel: float32 [2048, 1024], P('row', ('col', 'pblk'))
Inputs may be any that keep to these rules, and one draw needn't show every extreme that they name: `assign`: every one of the 4 blocks is named by exactly 2 layers.
All inputs are finite; a program needn't handle non-finite values.
Results may differ from a plain program's by a relative error of at most 0.00036.
Values may be sent and summed in bfloat16 or wider, within the bound.
No kernel may reach another device: no remote copies, remote signals or barrier semaphores. Data moves between devices by JAX's collectives and lax.ppermute only.
A program may use at most 128 MiB of HBM per device.

v0:
```python
import jax
import jax.numpy as jnp
from jax import lax
from jax.sharding import Mesh, PartitionSpec as P

SEQ = 64
NFEAT = 4
VOCAB = 256
LAYERS = 8
PR = 128
PS = 128


def shift_wide(inputs):
    blank = jnp.zeros_like(inputs[:, :1])
    earlier = jnp.concatenate([blank, inputs[:, :-1]], 1)
    later_cells = jnp.concatenate([inputs[:, 1:], blank], 1)
    return jnp.concatenate([earlier, inputs, later_cells], 2)


def panels(features, embed, conv_w, head, assign, proj_delta, proj_input):
    examples = features.shape[0]
    blocks_here = proj_delta.shape[0]
    offsets = jnp.arange(NFEAT, dtype=jnp.int32) * VOCAB
    table_rows = features.reshape(examples, SEQ, NFEAT) + offsets
    table_ids = jnp.arange(NFEAT * VOCAB, dtype=jnp.int32)
    onehot = (table_rows[:, :, 0:1] == table_ids).astype(jnp.bfloat16)
    for field in range(1, NFEAT):
        onehot = onehot + (table_rows[:, :, field : field + 1] == table_ids).astype(jnp.bfloat16)
    hidden = jnp.einsum("esv,vc->esc", onehot, embed, preferred_element_type=jnp.float32)
    wides = []
    pres = []
    for layer in range(LAYERS):
        wide_input = shift_wide(hidden.astype(jnp.bfloat16))
        pre_act = jnp.einsum(
            "esk,kc->esc", wide_input, conv_w[layer], preferred_element_type=jnp.float32
        )
        wides.append(wide_input)
        pres.append(pre_act)
        hidden = hidden + jax.nn.silu(pre_act)
    grad_h = jnp.broadcast_to(head / SEQ, hidden.shape)
    block_ids = jnp.arange(blocks_here, dtype=jnp.int32)
    panel = jnp.zeros((examples, blocks_here, PR, PS), jnp.float32)
    for layer in range(LAYERS - 1, -1, -1):
        pre_act = pres[layer]
        sigmoid_z = jax.nn.sigmoid(pre_act)
        delta_low = (grad_h * sigmoid_z * (1.0 + pre_act * (1.0 - sigmoid_z))).astype(jnp.bfloat16)
        block_pick = (assign[layer] == block_ids).astype(jnp.float32)
        rows_table = jnp.einsum("b,bcr->cr", block_pick, proj_delta.astype(jnp.float32)).astype(
            jnp.bfloat16
        )
        cols_table = jnp.einsum("b,bkt->kt", block_pick, proj_input.astype(jnp.float32)).astype(
            jnp.bfloat16
        )
        left_side = jnp.einsum(
            "esc,cr->esr", delta_low, rows_table, preferred_element_type=jnp.float32
        )
        right_side = jnp.einsum(
            "esk,kt->est", wides[layer], cols_table, preferred_element_type=jnp.float32
        )
        projected = jnp.einsum(
            "esr,est->ert", left_side, right_side, precision=lax.Precision.HIGHEST
        )
        panel = panel + block_pick[None, :, None, None] * projected[:, None]
        if layer > 0:
            back_wide = jnp.einsum(
                "esc,kc->esk", delta_low, conv_w[layer], preferred_element_type=jnp.float32
            )
            width = grad_h.shape[2]
            first_third = back_wide[:, :, :width]
            last_third = back_wide[:, :, 2 * width :]
            blank = jnp.zeros_like(first_third[:, :1])
            grad_input = back_wide[:, :, width : 2 * width]
            grad_input = grad_input + jnp.concatenate([first_third[:, 1:], blank], 1)
            grad_input = grad_input + jnp.concatenate([blank, last_third[:, :-1]], 1)
            grad_h = grad_h + grad_input
    return panel.reshape(examples, blocks_here, PR * PS).astype(jnp.bfloat16)


def on_device(left_feat, right_feat, embed, conv_w, head, assign, proj_delta, proj_input):
    group = ("zh", "core", "col")
    n_group = lax.axis_size(group)
    n_zh = lax.axis_size("zh")
    n_core = lax.axis_size("core")
    n_col = lax.axis_size("col")
    n_y = lax.axis_size("y")
    n_blk = lax.axis_size("pblk")
    left_each = left_feat.shape[0]
    right_each = right_feat.shape[2]
    right_local = right_feat.reshape(right_each, right_feat.shape[3])
    own_features = jnp.concatenate([left_feat, right_local], 0)
    panel = panels(own_features, embed, conv_w, head, assign, proj_delta, proj_input)
    own = panel.shape[0]
    width = panel.shape[1] * panel.shape[2] // n_group
    sliced = panel.reshape(own, n_group, width)
    spread = lax.all_to_all(sliced, group, split_axis=1, concat_axis=0, tiled=True)
    spread = spread.reshape(n_group, own, width)
    left_part = spread[:, :left_each].reshape(n_group * left_each, width)
    right_part = spread[:, left_each:].reshape(n_group * right_each, width)
    left_tile = lax.all_gather(left_part, "pblk", axis=0, tiled=True)
    right_tile = lax.all_gather(right_part, "y", axis=0, tiled=True)
    partial_tile = jnp.einsum(
        "lk,rk->lr", left_tile, right_tile, preferred_element_type=jnp.float32
    )
    partial_tile = partial_tile.reshape(
        n_blk, n_zh, n_core, n_col, left_each, n_y, n_zh, n_core, n_col, right_each
    )
    chunks = jnp.transpose(partial_tile, (1, 2, 8, 3, 0, 4, 6, 5, 7, 9))
    chunks = chunks.reshape(n_group, n_col * n_blk * left_each, n_zh * n_y * n_core * right_each)
    block = lax.psum_scatter(chunks, group, scatter_dimension=0, tiled=True)
    return block.reshape(block.shape[1], block.shape[2])


def solution(mesh):
    n_row = mesh.shape["row"]
    fine = Mesh(
        mesh.devices.reshape(2, 4, n_row // 8, mesh.shape["col"], mesh.shape["pblk"]),
        ("zh", "y", "core", "col", "pblk"),
    )
    rows = ("zh", "y", "core")
    placed = (
        P((*rows, "col", "pblk"), None),
        P("col", "pblk", rows, None),
        P(),
        P(),
        P(),
        P(),
        P(),
        P(),
    )
    return jax.shard_map(
        on_device, mesh=fine, in_specs=placed, out_specs=P(rows, ("col", "pblk")), check_vma=False
    )
```

profile of v0, /device:TPU:1, one launch (start us, length us, event | category | flops | bytes accessed | tf_op | source)
XLA Modules:
  0.0 414.9 jit_solution(5127504593989071444)
XLA Ops:
  37.8 2.8 fusion.262
  87.6 5.2 %mul.371 = f32[12,16,4096]{2,1,0:T(8,128)} reshape(f32[12,4,16384]{2,1,0:T(4,128)} %mul.370) | data formatting | bytes 6291456 | tf_op jit(solution)/shard_map/mul | solution.py:64
  92.8 3.7 mul.360
  96.5 5.2 %mul.361 = f32[12,16,4096]{2,1,0:T(8,128)} reshape(f32[12,4,16384]{2,1,0:T(4,128)} %mul.360) | data formatting | bytes 6291456 | tf_op jit(solution)/shard_map/mul | solution.py:64
  101.7 3.7 mul.350
  105.4 5.4 %mul.351 = f32[12,16,4096]{2,1,0:T(8,128)} reshape(f32[12,4,16384]{2,1,0:T(4,128)} %mul.350) | data formatting | bytes 6291456 | tf_op jit(solution)/shard_map/mul | solution.py:64
  110.8 3.6 mul.340
  114.4 5.3 %mul.341 = f32[12,16,4096]{2,1,0:T(8,128)} reshape(f32[12,4,16384]{2,1,0:T(4,128)} %mul.340) | data formatting | bytes 6291456 | tf_op jit(solution)/shard_map/mul | solution.py:64
  119.7 3.6 mul.330
  123.3 5.3 %mul.331 = f32[12,16,4096]{2,1,0:T(8,128)} reshape(f32[12,4,16384]{2,1,0:T(4,128)} %mul.330) | data formatting | bytes 6291456 | tf_op jit(solution)/shard_map/mul | solution.py:64
  128.6 3.7 mul.320
  132.2 5.2 %mul.321 = f32[12,16,4096]{2,1,0:T(8,128)} reshape(f32[12,4,16384]{2,1,0:T(4,128)} %mul.320) | data formatting | bytes 6291456 | tf_op jit(solution)/shard_map/mul | solution.py:64
  137.5 2.4 mul.310
  139.9 5.2 %mul.311 = f32[12,16,4096]{2,1,0:T(8,128)} reshape(f32[12,4,16384]{2,1,0:T(4,128)} %mul.310) | data formatting | bytes 6291456 | tf_op jit(solution)/shard_map/mul | solution.py:64
  147.5 5.3 %mul.301 = f32[12,16,4096]{2,1,0:T(8,128)} reshape(f32[12,4,16384]{2,1,0:T(4,128)} %mul.300) | data formatting | bytes 6291456 | tf_op jit(solution)/shard_map/mul | solution.py:64
  152.8 9.6 %add_convert_fusion = bf16[12,16,4096]{2,1,0:T(8,128)(2,1)S(1)} fusion(f32[12,16,4096]{2,1,0:T(8,128)} %mul.371, f32[12,16,4096]{2,1,0:T(8,128)} %mul.361, f32[12,16,4096]{2,1,0:T(8,128)} %mul.351, f32[12,16,4096]{2,1,0:T(8,128)} %mul.341, f32[12,16,4096]{2,1,0:T(8,128)} %mul.331, f32[12,16,4096]{2,1,0:T(8,128)} %mul.321, f32[12,16,4096]{2,1,0:T(8,128)} %mul.311, ...), kind=kLoop, calls=%fused_computation | loop fusion | flops 12582912 | bytes 26739200 | tf_op jit(solution)/shard_map/convert_element_type | solution.py:77
  163.3 57.9 %all_to_all.15 = bf16[12,16,4096]{2,0,1:T(8,128)(2,1)S(1)} all-to-all(bf16[12,16,4096]{2,0,1:T(8,128)(2,1)S(1)} %copy.40), channel_id=1, replica_groups=mesh['zh'=2,'y'=4,'core'=2,'col'=4,'pblk'=4] {'zh','core','col'}, dimensions={1} | all-to-all | bytes 3145728 | tf_op jit(solution)/shard_map/all_to_all | solution.py:96
  223.6 31.7 %all-gather.5.cloned.1.call-done = bf16[256,4096]{1,0:T(8,128)(2,1)} async-done(((bf16[64,4096]{1,0:T(8,128)(2,1)}), bf16[256,4096]{1,0:T(8,128)(2,1)}) %all-gather.5.cloned.1.call-update) | async-done | bytes 2097168 | tf_op jit(solution)/shard_map/all_gather | solution.py:101
  255.3 52.6 %all-gather.3.cloned.1.call-done = bf16[512,4096]{1,0:T(8,128)(2,1)} async-done(((bf16[128,4096]{1,0:T(8,128)(2,1)}), bf16[512,4096]{1,0:T(8,128)(2,1)}) %all-gather.3.cloned.1.call-update) | async-done | bytes 4194320 | tf_op jit(solution)/shard_map/all_gather | solution.py:100
  307.9 4.2 %fusion.271 = f32[512,256]{0,1:T(8,128)S(1)} fusion(bf16[512,4096]{1,0:T(8,128)(2,1)} %all-gather.3.cloned.1.call-done, bf16[256,4096]{1,0:T(8,128)(2,1)} %all-gather.5.cloned.1.call-done), kind=kOutput, calls=%fused_computation.291 | convolution fusion | flops 1073741824 | bytes 6815744 | tf_op jit(solution)/shard_map/lk,rk->lr/dot_general | solution.py:102
  312.1 11.5 %reshape.113 = f32[4,2,2,4,8,4,2,2,4,4]{4,3,2,1,0,9,8,7,6,5:T(4,128)} reshape(f32[512,256]{0,1:T(8,128)S(1)} %fusion.271) | data formatting | bytes 1048576 | tf_op jit(solution)/shard_map/reshape | solution.py:105
  323.6 9.9 %copy.42 = f32[2,2,4,4,4,8,2,4,2,4]{5,4,3,9,8,7,6,2,1,0:T(4,128)} copy(f32[2,2,4,4,4,8,2,4,2,4]{5,3,1,0,4,9,2,8,6,7:T(4,128)} %bitcast.292) | data formatting | bytes 1048576 | tf_op jit(solution)/shard_map/transpose | solution.py:108
  333.5 11.1 %reshape.114 = f32[16,128,64]{1,2,0:T(8,128)} reshape(f32[2,2,4,4,4,8,2,4,2,4]{5,4,3,9,8,7,6,2,1,0:T(4,128)} %copy.42) | data formatting | bytes 1048576 | tf_op jit(solution)/shard_map/reshape | solution.py:109
  344.6 63.3 %reduce-scatter.2.cloned.1.call-done = f32[1,128,64]{1,2,0:T(8,128)} async-done(((f32[16,128,64]{1,2,0:T(8,128)}), f32[1,128,64]{1,2,0:T(8,128)}) %reduce-scatter.2.cloned.1.call-update) | async-done | bytes 32784 | tf_op jit(solution)/shard_map/reduce_scatter | solution.py:110
  (165 shorter events, 83.2 us)
Async XLA Ops:
  6.5 31.3 %copy-start = (bf16[1024,256]{1,0:T(8,128)(2,1)S(1)}, bf16[1024,256]{1,0:T(8,128)(2,1)}, u32[]{:S(2)}) copy-start(bf16[1024,256]{1,0:T(8,128)(2,1)} %param.10) | copy-start | bytes 1572868
  6.5 15.2 %copy-start.3 = (bf16[4,768,128]{2,1,0:T(8,128)(2,1)S(1)}, bf16[4,768,128]{2,1,0:T(8,128)(2,1)}, u32[]{:S(2)}) copy-start(bf16[4,768,128]{2,1,0:T(8,128)(2,1)} %param.15) | copy-start | bytes 2359300
  6.5 248.8 %all-gather.5.cloned.1.call-start = ((), (), s32[]{:S(2)}) async-start(), calls=%async_computation.3 | async-start | bytes 2621440 | tf_op jit(solution)/shard_map/all_gather | solution.py:101
  32.1 3.6 copy-start.6
  32.1 4.8 %copy-start.4 = (s32[8,256]{1,0:T(8,128)S(1)}, s32[8,256]{1,0:T(8,128)}, u32[]{:S(2)}) copy-start(s32[8,256]{1,0:T(8,128)} %param.8) | copy-start | bytes 24580
  32.1 5.0 %copy-start.5 = (s32[1,1,4,256]{3,2,1,0:T(4,128)S(1)}, s32[1,1,4,256]{3,2,1,0:T(4,128)}, u32[]{:S(2)}) copy-start(s32[1,1,4,256]{3,2,1,0:T(4,128)} %param.9) | copy-start | bytes 12292
  37.8 3.0 copy-start.11
  40.8 1.9 copy-start.2
  42.7 1.0 copy-start.10
  44.2 1.0 copy-start.9
  45.6 1.0 copy-start.8
  47.1 1.0 copy-start.7
  222.5 85.5 %all-gather.3.cloned.1.call-start = ((), (), s32[]{:S(2)}) async-start(), calls=%async_computation.2 | async-start | bytes 5242880 | tf_op jit(solution)/shard_map/all_gather | solution.py:100
  223.6 184.3 %reduce-scatter.2.cloned.1.call-start = ((), (), s32[]{:S(2)}) async-start(), calls=%async_computation.4 | async-start | bytes 557056 | tf_op jit(solution)/shard_map/reduce_scatter | solution.py:110
  333.5 74.4 %copy-start.1 = (bf16[1024,256]{1,0:T(8,128)(2,1)S(1)}, bf16[1024,256]{1,0:T(8,128)(2,1)}, u32[]{:S(2)}) copy-start(bf16[1024,256]{1,0:T(8,128)(2,1)} %param.10) | copy-start | bytes 1572868
Sparse Core Ops, SparseCore 0:
  222.6 32.7 all-gather.4
  257.1 50.7 all-gather.2
  344.8 63.1 reduce-scatter.1
where the time goes:
time: 422 us; the launch traced here: 415 us
  waiting for transfers between devices  148 us (35%)
  local copies, waits for them, and re-layouts  124 us (29%)
  blocking collectives  57.9 us (14%)
  matrix products  53.7 us (13%)
  other arithmetic  17.5 us (4%)
  between operations  14.3 us (3%)
    mul x32, local copies, waits for them, and re-layouts, panels(): panel = panel + block_pick[None, :, None, None] * projected[:, None]  68.9 us
    reduce_scatter x1, waiting for transfers between devices, on_device(): block = lax.psum_scatter(chunks, group, scatter_dimension=0, tiled=True)  63.3 us
    all_to_all x1, blocking collectives, on_device(): lax.all_to_all(sliced, group, split_axis=1, concat_axis=0, tiled=True)  57.9 us
    all_gather x1, waiting for transfers between devices, on_device(): left_tile = lax.all_gather(left_part, 'pblk', axis=0, tiled=True)  52.6 us
    all_gather x1, waiting for transfers between devices, on_device(): right_tile = lax.all_gather(right_part, 'y', axis=0, tiled=True)  31.7 us
    unnamed x43, local copies, waits for them, and re-layouts  14.8 us
    dot_general x8, matrix products, panels(): jnp.einsum('b,bkt->kt', block_pick, proj_input.astype(jnp.float32))  13.3 us
    reshape x1, local copies, waits for them, and re-layouts, on_device(): partial_tile.reshape(n_blk, n_zh, n_core, n_col, left_each, n_y, n_zh, n_...  11.5 us
  transfers between devices with their start and end apart: 3, of which 3 were waited for; matrix products, arithmetic and copies ran while one was open for 0% of the time, Pallas kernels for 0%

commit v1 on v0

--- a/solution.py
+++ b/solution.py
@@ -9,6 +9,32 @@
 LAYERS = 8
 PR = 128
 PS = 128
+
+
+def ring_apply(x, axis, dim, work, out_dim):
+    size, mine, rows = (lax.axis_size(axis), lax.axis_index(axis), x.shape[dim])
+    right = [(i, (i + 1) % size) for i in range(size)]
+    behind = [(b, a) for a, b in right]
+    lower, upper = (lax.ppermute(x, axis, right), lax.ppermute(x, axis, behind))
+    made = work(x, mine * rows)
+    length = made.shape[out_dim]
+    filled = jnp.zeros(
+        (*made.shape[:out_dim], size * length, *made.shape[out_dim + 1 :]), made.dtype
+    )
+
+    def put(filled, made, owner):
+        return lax.dynamic_update_slice_in_dim(filled, made, owner * length, axis=out_dim)
+
+    filled = put(filled, made, mine)
+    for step in range(1, size // 2 + 1):
+        below, above = ((mine - step) % size, (mine + step) % size)
+        held = (lower, upper)
+        if step < size // 2:
+            lower, upper = (lax.ppermute(lower, axis, right), lax.ppermute(upper, axis, behind))
+        filled = put(filled, work(held[0], below * rows), below)
+        if 2 * step < size:
+            filled = put(filled, work(held[1], above * rows), above)
+    return filled
 
 
 def shift_wide(inputs):
@@ -97,10 +123,15 @@
     spread = spread.reshape(n_group, own, width)
     left_part = spread[:, :left_each].reshape(n_group * left_each, width)
     right_part = spread[:, left_each:].reshape(n_group * right_each, width)
-    left_tile = lax.all_gather(left_part, "pblk", axis=0, tiled=True)
     right_tile = lax.all_gather(right_part, "y", axis=0, tiled=True)
-    partial_tile = jnp.einsum(
-        "lk,rk->lr", left_tile, right_tile, preferred_element_type=jnp.float32
+    partial_tile = ring_apply(
+        left_part,
+        "pblk",
+        0,
+        lambda own_block, at: jnp.einsum(
+            "lk,rk->lr", own_block, right_tile, preferred_element_type=jnp.float32
+        ),
+        0,
     )
     partial_tile = partial_tile.reshape(
         n_blk, n_zh, n_core, n_col, left_each, n_y, n_zh, n_core, n_col, right_each

time: 422 us -> 391 us (0.927)
  waiting for transfers between devices: 148 us -> 104 us
  matrix products: 53.7 us -> 69.4 us
  local copies, waits for them, and re-layouts: 124 us -> 115 us
    all_gather x1 -> x0, waiting for transfers between devices: 52.6 us -> none  [on_device(): left_tile = lax.all_gather(left_part, 'pblk', axis=0, tiled=True)]
    ppermute x0 -> x3, waiting for transfers between devices: none -> 35.7 us  [the longest x2 23 us: ring_apply(): lower, upper = (lax.ppermute(x, axis, right), lax.ppermute(x, axis, behind))]
    all_gather x1, waiting for transfers between devices: 31.7 us -> 5.86 us  [on_device(): right_tile = lax.all_gather(right_part, 'y', axis=0, tiled=True)]
    dot_general x8, matrix products: 3.85 us -> 9.74 us  [panels(): jnp.einsum('esk,kt->est', wides[layer], cols_table, preferred_element_typ...]
    mul x32, local copies, waits for them, and re-layouts: 68.9 us -> 63.5 us  [panels(): panel = panel + block_pick[None, :, None, None] * projected[:, None]]
    unnamed x43 -> x123, local copies, waits for them, and re-layouts: 14.8 us -> 11.9 us
  transfers between devices with their start and end apart: 3 -> 5, of which waited for: 3 -> 4; matrix products, arithmetic and copies ran while one was open for 0% -> 2% of each run, Pallas kernels for 0% -> 0%
where the time goes in v1:
time: 391 us; the launch traced here: 383 us
  local copies, waits for them, and re-layouts  115 us (29%)
  waiting for transfers between devices  104 us (27%)
  matrix products  69.4 us (18%)
  blocking collectives  57.9 us (15%)
  other arithmetic  19.3 us (5%)
  between operations  14.9 us (4%)
    mul x32, local copies, waits for them, and re-layouts, panels(): panel = panel + block_pick[None, :, None, None] * projected[:, None]  63.5 us
    reduce_scatter x1, waiting for transfers between devices, on_device(): block = lax.psum_scatter(chunks, group, scatter_dimension=0, tiled=True)  62 us
    all_to_all x1, blocking collectives, on_device(): lax.all_to_all(sliced, group, split_axis=1, concat_axis=0, tiled=True)  57.9 us
    ppermute x2, waiting for transfers between devices, ring_apply(): lower, upper = (lax.ppermute(x, axis, right), lax.ppermute(x, axis, behind))  23 us
    dot_general x8, matrix products, panels(): jnp.einsum('b,bkt->kt', block_pick, proj_input.astype(jnp.float32))  15.3 us
    ppermute x1, waiting for transfers between devices, ring_apply(): lax.ppermute(lower, axis, right)  12.7 us
    unnamed x123, local copies, waits for them, and re-layouts  11.9 us
    dot_general x8, matrix products, panels(): jnp.einsum('esr,est->ert', left_side, right_side, precision=lax.Precision...  11.3 us
  transfers between devices with their start and end apart: 5, of which 4 were waited for; matrix products, arithmetic and copies ran while one was open for 2% of the time, Pallas kernels for 0%

profile of v1, /device:TPU:1, one launch (start us, length us, event | category | flops | bytes accessed | tf_op | source)
XLA Modules:
  0.0 383.5 jit_solution(16439235554031140274)
XLA Ops:
  45.3 2.8 fusion.262
  68.4 2.4 mul.382
  70.9 5.2 %mul.383 = f32[12,16,4096]{2,1,0:T(8,128)} reshape(f32[12,4,16384]{2,1,0:T(4,128)} %mul.382) | data formatting | bytes 6291456 | tf_op jit(solution)/shard_map/mul | solution.py:90
  80.3 2.5 mul.372
  82.8 5.3 %mul.373 = f32[12,16,4096]{2,1,0:T(8,128)} reshape(f32[12,4,16384]{2,1,0:T(4,128)} %mul.372) | data formatting | bytes 6291456 | tf_op jit(solution)/shard_map/mul | solution.py:90
  92.2 2.5 mul.362
  94.7 5.4 %mul.363 = f32[12,16,4096]{2,1,0:T(8,128)} reshape(f32[12,4,16384]{2,1,0:T(4,128)} %mul.362) | data formatting | bytes 6291456 | tf_op jit(solution)/shard_map/mul | solution.py:90
  106.7 5.4 %mul.353 = f32[12,16,4096]{2,1,0:T(8,128)} reshape(f32[12,4,16384]{2,1,0:T(4,128)} %mul.352) | data formatting | bytes 6291456 | tf_op jit(solution)/shard_map/mul | solution.py:90
  118.4 5.3 %mul.343 = f32[12,16,4096]{2,1,0:T(8,128)} reshape(f32[12,4,16384]{2,1,0:T(4,128)} %mul.342) | data formatting | bytes 6291456 | tf_op jit(solution)/shard_map/mul | solution.py:90
  130.1 5.5 %mul.333 = f32[12,16,4096]{2,1,0:T(8,128)} reshape(f32[12,4,16384]{2,1,0:T(4,128)} %mul.332) | data formatting | bytes 6291456 | tf_op jit(solution)/shard_map/mul | solution.py:90
  138.5 2.5 mul.322
  141.0 5.3 %mul.323 = f32[12,16,4096]{2,1,0:T(8,128)} reshape(f32[12,4,16384]{2,1,0:T(4,128)} %mul.322) | data formatting | bytes 6291456 | tf_op jit(solution)/shard_map/mul | solution.py:90
  149.2 2.4 mul.312
  151.7 5.3 %mul.313 = f32[12,16,4096]{2,1,0:T(8,128)} reshape(f32[12,4,16384]{2,1,0:T(4,128)} %mul.312) | data formatting | bytes 6291456 | tf_op jit(solution)/shard_map/mul | solution.py:90
  158.2 9.6 %add_convert_fusion = bf16[12,16,4096]{2,1,0:T(8,128)(2,1)S(1)} fusion(f32[12,16,4096]{2,1,0:T(8,128)} %mul.383, f32[12,16,4096]{2,1,0:T(8,128)} %mul.373, f32[12,16,4096]{2,1,0:T(8,128)} %mul.363, f32[12,16,4096]{2,1,0:T(8,128)} %mul.353, f32[12,16,4096]{2,1,0:T(8,128)} %mul.343, f32[12,16,4096]{2,1,0:T(8,128)} %mul.333, f32[12,16,4096]{2,1,0:T(8,128)} %mul.323, ...), kind=kLoop, calls=%fused_computation | loop fusion | flops 12582912 | bytes 26739200 | tf_op jit(solution)/shard_map/convert_element_type | solution.py:103
  168.8 57.9 %all_to_all.15 = bf16[12,16,4096]{2,0,1:T(8,128)(2,1)S(1)} all-to-all(bf16[12,16,4096]{2,0,1:T(8,128)(2,1)S(1)} %copy.48), channel_id=1, replica_groups=mesh['zh'=2,'y'=4,'core'=2,'col'=4,'pblk'=4] {'zh','core','col'}, dimensions={1} | all-to-all | bytes 3145728 | tf_op jit(solution)/shard_map/all_to_all | solution.py:122
  231.9 23.0 %collective-permute-done = bf16[128,4096]{1,0:T(8,128)(2,1)} collective-permute-done((bf16[128,4096]{1,0:T(8,128)(2,1)}, bf16[128,4096]{1,0:T(8,128)(2,1)}, u32[]{:S(2)}, u32[]{:S(2)}) %collective-permute-start) | collective-permute-done | bytes 1048608 | tf_op jit(solution)/shard_map/ppermute | solution.py:18
  254.9 5.9 %all-gather.2.cloned.1.call-done = bf16[256,4096]{1,0:T(8,128)(2,1)} async-done(((bf16[64,4096]{1,0:T(8,128)(2,1)}), bf16[256,4096]{1,0:T(8,128)(2,1)}) %all-gather.2.cloned.1.call-update) | async-done | bytes 2097168 | tf_op jit(solution)/shard_map/all_gather | solution.py:126
  260.8 2.4 convolution_dynamic-update-slice_fusion.3
  267.1 12.7 %collective-permute-done.2 = bf16[128,4096]{1,0:T(8,128)(2,1)} collective-permute-done((bf16[128,4096]{1,0:T(8,128)(2,1)}, bf16[128,4096]{1,0:T(8,128)(2,1)}, u32[]{:S(2)}, u32[]{:S(2)}) %collective-permute-start.2) | collective-permute-done | bytes 1048608 | tf_op jit(solution)/shard_map/ppermute | solution.py:33
  281.8 11.3 %reshape.113 = f32[4,2,2,4,8,4,2,2,4,4]{4,3,2,1,0,9,8,7,6,5:T(4,128)} reshape(f32[512,256]{0,1:T(8,128)S(1)} %convolution_dynamic-update-slice_fusion) | data formatting | bytes 1048576 | tf_op jit(solution)/shard_map/reshape | solution.py:136
  293.1 10.0 %copy.53 = f32[2,2,4,4,4,8,2,4,2,4]{5,4,3,9,8,7,6,2,1,0:T(4,128)} copy(f32[2,2,4,4,4,8,2,4,2,4]{5,3,1,0,4,9,2,8,6,7:T(4,128)} %bitcast.298) | data formatting | bytes 1048576 | tf_op jit(solution)/shard_map/transpose | solution.py:139
  303.1 11.1 %reshape.114 = f32[16,128,64]{1,2,0:T(8,128)} reshape(f32[2,2,4,4,4,8,2,4,2,4]{5,4,3,9,8,7,6,2,1,0:T(4,128)} %copy.53) | data formatting | bytes 1048576 | tf_op jit(solution)/shard_map/reshape | solution.py:140
  314.2 62.0 %reduce-scatter.2.cloned.1.call-done = f32[1,128,64]{1,2,0:T(8,128)} async-done(((f32[16,128,64]{1,2,0:T(8,128)}), f32[1,128,64]{1,2,0:T(8,128)}) %reduce-scatter.2.cloned.1.call-update) | async-done | bytes 32784 | tf_op jit(solution)/shard_map/reduce_scatter | solution.py:141
  (252 shorter events, 104.7 us)
Async XLA Ops:
  6.5 38.7 %copy-start = (bf16[1024,256]{1,0:T(8,128)(2,1)S(1)}, bf16[1024,256]{1,0:T(8,128)(2,1)}, u32[]{:S(2)}) copy-start(bf16[1024,256]{1,0:T(8,128)(2,1)} %param.10) | copy-start | bytes 1572868
  6.5 254.2 %all-gather.2.cloned.1.call-start = ((), (), s32[]{:S(2)}) async-start(), calls=%async_computation.2 | async-start | bytes 2621440 | tf_op jit(solution)/shard_map/all_gather | solution.py:126
  31.8 12.6 %copy-start.42 = (s32[1,1,4,256]{3,2,1,0:T(4,128)S(1)}, s32[1,1,4,256]{3,2,1,0:T(4,128)}, u32[]{:S(2)}) copy-start(s32[1,1,4,256]{3,2,1,0:T(4,128)} %param.9) | copy-start | bytes 12292
  31.8 12.8 %copy-start.41 = (s32[8,256]{1,0:T(8,128)S(1)}, s32[8,256]{1,0:T(8,128)}, u32[]{:S(2)}) copy-start(s32[8,256]{1,0:T(8,128)} %param.8) | copy-start | bytes 24580
  94.7 5.7 %copy-start.11 = (bf16[12,64,256]{2,1,0:T(8,128)(2,1)S(1)}, bf16[12,64,256]{2,1,0:T(8,128)(2,1)}, u32[]{:S(2)}) copy-start(bf16[12,64,256]{2,1,0:T(8,128)(2,1)} %copy-done.10) | copy-start | bytes 1179652
  106.7 5.6 %copy-start.9 = (bf16[12,64,256]{2,1,0:T(8,128)(2,1)S(1)}, bf16[12,64,256]{2,1,0:T(8,128)(2,1)}, u32[]{:S(2)}) copy-start(bf16[12,64,256]{2,1,0:T(8,128)(2,1)} %copy-done.8) | copy-start | bytes 1179652
  106.7 5.6 %copy-start.28 = (bf16[12,63,256]{2,1,0:T(8,128)(2,1)S(1)}, bf16[12,63,256]{2,1,0:T(8,128)(2,1)}, u32[]{:S(2)}) copy-start(bf16[12,63,256]{2,1,0:T(8,128)(2,1)} %copy-done.27) | copy-start | bytes 1161220
  118.4 5.6 %copy-start.7 = (bf16[12,64,256]{2,1,0:T(8,128)(2,1)S(1)}, bf16[12,64,256]{2,1,0:T(8,128)(2,1)}, u32[]{:S(2)}) copy-start(bf16[12,64,256]{2,1,0:T(8,128)(2,1)} %copy-done.6) | copy-start | bytes 1179652
  118.4 5.6 %copy-start.24 = (bf16[12,63,256]{2,1,0:T(8,128)(2,1)S(1)}, bf16[12,63,256]{2,1,0:T(8,128)(2,1)}, u32[]{:S(2)}) copy-start(bf16[12,63,256]{2,1,0:T(8,128)(2,1)} %copy-done.23) | copy-start | bytes 1161220
  118.4 5.6 %copy-start.26 = (bf16[12,63,256]{2,1,0:T(8,128)(2,1)S(1)}, bf16[12,63,256]{2,1,0:T(8,128)(2,1)}, u32[]{:S(2)}) copy-start(bf16[12,63,256]{2,1,0:T(8,128)(2,1)} %copy-done.25) | copy-start | bytes 1161220
  130.1 5.8 %copy-start.5 = (bf16[12,64,256]{2,1,0:T(8,128)(2,1)S(1)}, bf16[12,64,256]{2,1,0:T(8,128)(2,1)}, u32[]{:S(2)}) copy-start(bf16[12,64,256]{2,1,0:T(8,128)(2,1)} %copy-done.4) | copy-start | bytes 1179652
  130.1 5.8 %copy-start.20 = (bf16[12,63,256]{2,1,0:T(8,128)(2,1)S(1)}, bf16[12,63,256]{2,1,0:T(8,128)(2,1)}, u32[]{:S(2)}) copy-start(bf16[12,63,256]{2,1,0:T(8,128)(2,1)} %copy-done.19) | copy-start | bytes 1161220
  130.1 5.8 %copy-start.22 = (bf16[12,63,256]{2,1,0:T(8,128)(2,1)S(1)}, bf16[12,63,256]{2,1,0:T(8,128)(2,1)}, u32[]{:S(2)}) copy-start(bf16[12,63,256]{2,1,0:T(8,128)(2,1)} %copy-done.21) | copy-start | bytes 1161220
  130.1 5.9 %copy-start.49 = (f32[1,768,128]{2,0,1:T(1,128)S(1)}, f32[1,768,128]{2,0,1:T(1,128)}, u32[]{:S(2)}) copy-start(f32[1,768,128]{2,0,1:T(1,128)} %fusion.183) | copy-start | bytes 1179652
  141.0 5.6 %copy-start.16 = (bf16[12,63,256]{2,1,0:T(8,128)(2,1)S(1)}, bf16[12,63,256]{2,1,0:T(8,128)(2,1)}, u32[]{:S(2)}) copy-start(bf16[12,63,256]{2,1,0:T(8,128)(2,1)} %copy-done.15) | copy-start | bytes 1161220
  141.0 5.6 %copy-start.18 = (bf16[12,63,256]{2,1,0:T(8,128)(2,1)S(1)}, bf16[12,63,256]{2,1,0:T(8,128)(2,1)}, u32[]{:S(2)}) copy-start(bf16[12,63,256]{2,1,0:T(8,128)(2,1)} %copy-done.17) | copy-start | bytes 1161220
  141.0 5.6 %copy-start.48 = (f32[1,768,128]{2,0,1:T(1,128)S(1)}, f32[1,768,128]{2,0,1:T(1,128)}, u32[]{:S(2)}) copy-start(f32[1,768,128]{2,0,1:T(1,128)} %fusion.187) | copy-start | bytes 1179652
  151.7 5.7 %copy-start.45 = (f32[4]{0:T(128)S(1)}, f32[4]{0:T(128)}, u32[]{:S(2)}) copy-start(f32[4]{0:T(128)} %fusion.193) | copy-start | bytes 52
  151.7 5.8 %copy-start.44 = (f32[4]{0:T(128)S(1)}, f32[4]{0:T(128)}, u32[]{:S(2)}) copy-start(f32[4]{0:T(128)} %fusion.194) | copy-start | bytes 52
  227.9 148.3 %reduce-scatter.2.cloned.1.call-start = ((), (), s32[]{:S(2)}) async-start(), calls=%async_computation.3 | async-start | bytes 557056 | tf_op jit(solution)/shard_map/reduce_scatter | solution.py:141
  229.0 25.9 %collective-permute-start = (bf16[128,4096]{1,0:T(8,128)(2,1)}, bf16[128,4096]{1,0:T(8,128)(2,1)}, u32[]{:S(2)}, u32[]{:S(2)}) collective-permute-start(bf16[128,4096]{1,0:T(8,128)(2,1)} %slice_bitcast_fusion), channel_id=1, source_target_pairs={{0,1},{1,2},{2,3},{3,0},{4,5},{5,6},{6,7},{7,4},{8,9},{9,10},{10,1... | collective-permute-start | bytes 3145736 | tf_op jit(solution)/shard_map/ppermute | solution.py:18
  230.2 35.0 %collective-permute-start.1 = (bf16[128,4096]{1,0:T(8,128)(2,1)}, bf16[128,4096]{1,0:T(8,128)(2,1)}, u32[]{:S(2)}, u32[]{:S(2)}) collective-permute-start(bf16[128,4096]{1,0:T(8,128)(2,1)} %slice_bitcast_fusion), channel_id=1, source_target_pairs={{1,0},{2,1},{3,2},{0,3},{5,4},{6,5},{7,6},{4,7},{9,8},{10,9},{11,1... | collective-permute-start | bytes 3145736 | tf_op jit(solution)/shard_map/ppermute | solution.py:18
  254.9 25.0 %collective-permute-start.2 = (bf16[128,4096]{1,0:T(8,128)(2,1)}, bf16[128,4096]{1,0:T(8,128)(2,1)}, u32[]{:S(2)}, u32[]{:S(2)}) collective-permute-start(bf16[128,4096]{1,0:T(8,128)(2,1)} %collective-permute-done), channel_id=1, source_target_pairs={{0,1},{1,2},{2,3},{3,0},{4,5},{5,6},{6,7},{7,4},{8,9},{9,10},{10,1... | collective-permute-start | bytes 3145736 | tf_op jit(solution)/shard_map/ppermute | solution.py:33
  303.1 73.1 %copy-start.1 = (bf16[1024,256]{1,0:T(8,128)(2,1)S(1)}, bf16[1024,256]{1,0:T(8,128)(2,1)}, u32[]{:S(2)}) copy-start(bf16[1024,256]{1,0:T(8,128)(2,1)} %param.10) | copy-start | bytes 1572868
  (33 other events, 67.9 us)
Sparse Core Ops, SparseCore 0:
  228.0 32.6 all-gather.1
  314.3 61.8 reduce-scatter.1
